TPU v7x, 32 devices: a whole 2x2x4 slice. The times are simulated.
32 devices in a mesh: tile: 8 (over z, x), chan: 4 (over y, core).
Axes of the slice: x: 2, y: 2, z: 4, core: 2. Of those that a mesh axis runs over, the one named last changes fastest.
Arguments:
- visibilities: float32 [4, 2048, 128], P('chan', 'tile'), may hold values from -6 to 6
- kernels: bfloat16 [4, 32, 2, 64, 128], P('chan'), may hold values from -0.75 to 0.75
- destination: int32 [4, 2048, 1], P('chan', 'tile'), may hold values from 0 to 7; in each aligned block of 256 rows (0 to 255, 256 to 511, ..., all dimensions but the last counted through in order) at most 96 rows name the same one
- cell: int32 [4, 2048], P('chan', 'tile'), may hold values from 0 to 2047
- plane: int32 [4, 2048], P('chan', 'tile'), may hold values from 0 to 31
Outputs:
- image: float32 [1024, 1024], P('chan', 'tile')
Inputs may be any that keep to these rules, and one draw needn't show every extreme that they name: `destination`: in the rows of one device (aligned blocks of 256 rows), no tile is named more than 96 times; some tile is named exactly 96 times in some devices' rows.
All inputs are finite; a program needn't handle non-finite values.
Results may differ from a plain program's by a relative error of at most 0.0059.
Values may be sent and summed in bfloat16 or wider, within the bound.
No kernel may reach another device: no remote copies, remote signals or barrier semaphores. Data moves between devices by JAX's collectives and lax.ppermute only.
A program may use at most 384 MiB of HBM per device.

v0:
```python
import math

import jax
import jax.numpy as jnp
from jax import lax
from jax.sharding import PartitionSpec as P

G = 8192
S = 64
NW = 32
P_SIZE = 1024


def phase_tables(row_count, grid_width, pixels):
    spacing = grid_width // pixels - 1
    row_index = jnp.arange(row_count, dtype=jnp.int32)
    pixel_index = jnp.arange(pixels, dtype=jnp.int32)
    product = jnp.mod(
        (row_index[:, None] - grid_width // 2) * (spacing * (pixel_index[None, :] - pixels // 2)),
        grid_width,
    )
    phase_angle = product.astype(jnp.float32) * (2.0 * math.pi / grid_width)
    return (jnp.cos(phase_angle).astype(jnp.bfloat16), jnp.sin(phase_angle).astype(jnp.bfloat16))


def block_patches(samples, kernel_rows):
    sample_count = samples.shape[1] // 2
    support = kernel_rows.shape[3] // 2
    vis_real = samples[:, :sample_count, None]
    vis_imag = samples[:, sample_count:, None]
    kern_real = kernel_rows[:, 0, :, support:].astype(jnp.float32)
    kern_imag = kernel_rows[:, 1, :, support:].astype(jnp.float32)
    weighted_real = (vis_real * kern_real - vis_imag * kern_imag).astype(jnp.bfloat16)
    weighted_imag = (vis_real * kern_imag + vis_imag * kern_real).astype(jnp.bfloat16)
    u_kernel = kernel_rows[:, :, :, :support]
    v_weighted = jnp.stack(
        [
            jnp.stack([weighted_real, weighted_imag], 2),
            jnp.stack([-weighted_imag, weighted_real], 2),
        ],
        1,
    )
    return jnp.einsum("bpkx,bpkqy->bxqy", u_kernel, v_weighted, preferred_element_type=jnp.float32)


def local(visibilities, kernels, destination, cell, plane):
    tile_count = lax.axis_size("tile")
    tile_index = lax.axis_index("tile")
    samples = visibilities[0]
    kernel_set = kernels[0]
    owners = destination[0, :, 0]
    blocks = samples.shape[0]
    capacity = 3 * blocks // tile_count
    onehot = (owners[:, None] == jnp.arange(tile_count, dtype=jnp.int32)[None, :]).astype(jnp.int32)
    slot_rank = jnp.sum(jnp.cumsum(onehot, axis=0) * onehot, axis=1) - 1
    packed_meta = cell[0] * NW + plane[0]
    send_samples = (
        jnp.zeros((tile_count, capacity, samples.shape[1]), jnp.float32)
        .at[owners, slot_rank]
        .set(samples)
    )
    send_meta = jnp.zeros((tile_count, capacity), jnp.int32).at[owners, slot_rank].set(packed_meta)
    arrived, arrived_meta = (
        lax.all_to_all(send_samples, "tile", split_axis=0, concat_axis=0, tiled=True),
        lax.all_to_all(send_meta, "tile", split_axis=0, concat_axis=0, tiled=True),
    )
    slot_total = tile_count * capacity
    stride = math.gcd(slot_total, 256)
    arrived = arrived.reshape(slot_total // stride, stride, samples.shape[1])
    arrived_meta = arrived_meta.reshape(slot_total // stride, stride)
    slab_rows = G // tile_count
    cell_cols = G // S

    def add_block(grid_cells, blk):
        sample_blk, meta_blk = blk
        patches = block_patches(sample_blk, kernel_set[meta_blk % NW])
        return (grid_cells.at[meta_blk // NW].add(patches), None)

    grid_start = jnp.zeros((slab_rows // S * cell_cols, S, 2, S), jnp.float32)
    grid_cells, _ = lax.scan(add_block, grid_start, (arrived, arrived_meta))
    grid_round = grid_cells.astype(jnp.bfloat16).reshape(slab_rows // S, cell_cols, S, 2, S)
    cosine, sine = phase_tables(G, G, P_SIZE)
    with_cosine = jnp.einsum(
        "acxpy,cym->pmax",
        grid_round,
        cosine.reshape(cell_cols, S, P_SIZE),
        preferred_element_type=jnp.float32,
    ).reshape(2, P_SIZE, slab_rows)
    with_sine = jnp.einsum(
        "acxpy,cym->pmax",
        grid_round,
        sine.reshape(cell_cols, S, P_SIZE),
        preferred_element_type=jnp.float32,
    ).reshape(2, P_SIZE, slab_rows)
    transformed = jnp.stack([with_cosine[0] - with_sine[1], with_sine[0] + with_cosine[1]]).astype(
        jnp.bfloat16
    )
    own_cosine = lax.dynamic_slice_in_dim(cosine, tile_index * slab_rows, slab_rows, 0)
    own_sine = lax.dynamic_slice_in_dim(sine, tile_index * slab_rows, slab_rows, 0)
    columns = lax.psum_scatter(
        jnp.dot(transformed[0], own_cosine, preferred_element_type=jnp.float32)
        - jnp.dot(transformed[1], own_sine, preferred_element_type=jnp.float32),
        "tile",
        scatter_dimension=0,
        tiled=True,
    )
    summed = lax.psum_scatter(columns, "chan", scatter_dimension=1, tiled=True)
    return summed.T * (1.0 / G)


def solution(mesh):
    placed = (
        P("chan", "tile", None),
        P("chan", None, None, None, None),
        P("chan", "tile", None),
        P("chan", "tile"),
        P("chan", "tile"),
    )
    return jax.shard_map(
        local, mesh=mesh, in_specs=placed, out_specs=P("chan", "tile"), check_vma=False
    )
```

profile of v0, /device:TPU:0, one launch (start us, length us, event | category | flops | bytes accessed | tf_op | source)
XLA Modules:
  0.0 1180.5 jit_solution(10870274440548493141)
XLA Ops:
  10.8 38.6 %scatter_fusion.1 = s32[8,96]{1,0:T(8,128)} fusion(s32[8,96]{1,0:T(8,128)} %broadcast_in_dim.7, s32[256]{0:T(256)S(1)} %bitcast.135, s32[256]{0:T(256)S(1)} %bitcast.145), kind=kCustom, calls=%fused_computation.2 | custom fusion | bytes 5120 | tf_op jit(solution)/shard_map/scatter | solution.py:62
  49.4 7.3 all-to-all-start
  57.5 27.7 %scatter_fusion.2 = f32[8,96,128]{2,1,0:T(8,128)} fusion(f32[8,96,128]{2,1,0:T(8,128)} %broadcast_in_dim.8, s32[256]{0:T(256)S(1)} %bitcast.136, f32[256,128]{1,0:T(8,128)} %bitcast.140), kind=kCustom, calls=%fused_computation.3 | custom fusion | bytes 395264 | tf_op jit(solution)/shard_map/scatter | solution.py:60
  91.4 19.9 %fusion.15 = f32[8192,1024]{1,0:T(8,128)} fusion(s32[1024]{0:T(1024)S(1)} %add_multiply_fusion, s32[8192]{0:T(1024)S(1)} %iota_add_fusion), kind=kLoop, calls=%fused_computation.47 | loop fusion | flops 117440512 | bytes 33591296 | tf_op jit(solution)/shard_map/mul | solution.py:22
  113.0 41.3 %broadcast_in_dim.6 = f32[2048,64,2,64]{3,1,2,0:T(8,128)} broadcast(f32[]{:T(128)} %constant.115.clone.1), dimensions={} | broadcast | bytes 67108864 | tf_op jit(solution)/shard_map/broadcast_in_dim | solution.py:79
  154.3 300.1 %while.12 = (s32[]{:T(128)}, f32[2048,64,2,64]{3,1,2,0:T(8,128)}, s32[3,256]{1,0:T(4,128)S(1)}, bf16[32,2,64,128]{3,2,1,0:T(8,128)(2,1)S(1)}, f32[3,256,128]{2,1,0:T(8,128)S(1)}, /*index=5*/s32[]{:T(128)}) while((s32[]{:T(128)}, f32[2048,64,2,64]{3,1,2,0:T(8,128)}, s32[3,256]{1,0:T(4,128)S(1)}, bf16[32,2,64,128]{3,2,1,0:T(8,128)(2,1)S(1)}, ...), condition=%wide.region_7.8_spmd, body=%wide.region_5.7_spmd.sunk | while | flops 573579520 | bytes 122434688 | solution.py:80
  154.3 8.5 gather_fusion
  163.0 8.8 fusion.70
  171.9 7.1 fusion.71
  179.0 6.6 maximum_bitcast_fusion.3
  185.6 14.8 %fusion.72 = f32[256,64,2,64]{3,1,2,0:T(8,128)} fusion(bf16[256,1,64,2,64]{4,2,1,3,0:T(8,128)(2,1)} %get-tuple-element.141, bf16[256,1,64,2,64]{4,2,1,3,0:T(8,128)(2,1)} %get-tuple-element.142, bf16[256,2,64,128]{3,2,1,0:T(8,128)(2,1)} %gather_fusion), kind=kOutput, calls=%fused_computation.12.clone.1 | convolution fusion | flops 553648128 | bytes 25165824 | tf_op jit(solution)/shard_map/while/body/eval_jaxpr/bpkx,bpkqy->bxqy/dot_general | solution.py:43
  200.4 53.5 %scatter_fusion = f32[2048,64,2,64]{3,1,2,0:T(8,128)} fusion(f32[2048,64,2,64]{3,1,2,0:T(8,128)} %get-tuple-element.150, s32[256]{0:T(256)S(1)} %bitcast.141, f32[256,64,2,64]{3,1,2,0:T(8,128)} %fusion.72), kind=kCustom, calls=%fused_computation.1.clone.1 | custom fusion | flops 2097152 | bytes 25166848 | tf_op jit(solution)/shard_map/while/body/eval_jaxpr/scatter-add | solution.py:77
  254.0 8.5 gather_fusion
  262.6 8.8 fusion.70
  271.5 7.1 fusion.71
  278.6 6.6 maximum_bitcast_fusion.3
  285.2 14.8 %fusion.72 = f32[256,64,2,64]{3,1,2,0:T(8,128)} fusion(bf16[256,1,64,2,64]{4,2,1,3,0:T(8,128)(2,1)} %get-tuple-element.141, bf16[256,1,64,2,64]{4,2,1,3,0:T(8,128)(2,1)} %get-tuple-element.142, bf16[256,2,64,128]{3,2,1,0:T(8,128)(2,1)} %gather_fusion), kind=kOutput, calls=%fused_computation.12.clone.1 | convolution fusion | flops 553648128 | bytes 25165824 | tf_op jit(solution)/shard_map/while/body/eval_jaxpr/bpkx,bpkqy->bxqy/dot_general | solution.py:43
  300.0 53.9 %scatter_fusion = f32[2048,64,2,64]{3,1,2,0:T(8,128)} fusion(f32[2048,64,2,64]{3,1,2,0:T(8,128)} %get-tuple-element.150, s32[256]{0:T(256)S(1)} %bitcast.141, f32[256,64,2,64]{3,1,2,0:T(8,128)} %fusion.72), kind=kCustom, calls=%fused_computation.1.clone.1 | custom fusion | flops 2097152 | bytes 25166848 | tf_op jit(solution)/shard_map/while/body/eval_jaxpr/scatter-add | solution.py:77
  353.9 8.4 gather_fusion
  362.5 8.8 fusion.70
  371.4 7.1 fusion.71
  378.5 6.6 maximum_bitcast_fusion.3
  385.1 14.8 %fusion.72 = f32[256,64,2,64]{3,1,2,0:T(8,128)} fusion(bf16[256,1,64,2,64]{4,2,1,3,0:T(8,128)(2,1)} %get-tuple-element.141, bf16[256,1,64,2,64]{4,2,1,3,0:T(8,128)(2,1)} %get-tuple-element.142, bf16[256,2,64,128]{3,2,1,0:T(8,128)(2,1)} %gather_fusion), kind=kOutput, calls=%fused_computation.12.clone.1 | convolution fusion | flops 553648128 | bytes 25165824 | tf_op jit(solution)/shard_map/while/body/eval_jaxpr/bpkx,bpkqy->bxqy/dot_general | solution.py:43
  399.9 54.5 %scatter_fusion = f32[2048,64,2,64]{3,1,2,0:T(8,128)} fusion(f32[2048,64,2,64]{3,1,2,0:T(8,128)} %get-tuple-element.150, s32[256]{0:T(256)S(1)} %bitcast.141, f32[256,64,2,64]{3,1,2,0:T(8,128)} %fusion.72), kind=kCustom, calls=%fused_computation.1.clone.1 | custom fusion | flops 2097152 | bytes 25166848 | tf_op jit(solution)/shard_map/while/body/eval_jaxpr/scatter-add | solution.py:77
  454.4 63.8 %convert_element_type.143 = bf16[2048,64,2,64]{3,1,2,0:T(8,128)(2,1)} convert(f32[2048,64,2,64]{3,1,2,0:T(8,128)} %get-tuple-element.73) | non-fusion elementwise | flops 16777216 | bytes 100663296 | tf_op jit(solution)/shard_map/convert_element_type | solution.py:81
  518.2 105.0 %copy.23 = bf16[16,128,64,2,64]{1,2,4,3,0:T(8,128)(2,1)} copy(bf16[16,128,64,2,64]{4,2,3,1,0:T(8,128)(2,1)} %bitcast.31) | data formatting | bytes 67108864 | tf_op jit(solution)/shard_map/reshape | solution.py:81
  623.2 222.5 %fusion.28 = f32[2,1024,16,64]{1,3,0,2:T(8,128)S(1)} fusion(bf16[16,128,64,2,64]{1,2,4,3,0:T(8,128)(2,1)} %copy.23, s32[1024]{0:T(1024)S(1)} %copy-done.4, s32[128,64]{0,1:T(8,128)S(1)} %copy-done.2), kind=kOutput, calls=%fused_computation.62 | convolution fusion | flops 34485567488 | bytes 41979904 | tf_op jit(solution)/shard_map/acxpy,cym->pmax/dot_general | solution.py:89
  845.8 170.7 %fusion.31 = f32[2,1024,16,64]{1,3,0,2:T(8,128)} fusion(bf16[16,128,64,2,64]{1,2,4,3,0:T(8,128)(2,1)S(1)} %copy-done.1, s32[1024]{0:T(1024)S(1)} %copy-done.4, s32[128,64]{0,1:T(8,128)S(1)} %copy-done.2), kind=kOutput, calls=%fused_computation.63 | convolution fusion | flops 34485567488 | bytes 41979904 | tf_op jit(solution)/shard_map/acxpy,cym->pmax/dot_general | solution.py:83
  1020.7 17.0 %fusion.34 = f32[1024,1024]{1,0:T(8,128)S(1)} fusion(bf16[1024,1024]{0,1:T(8,128)(2,1)S(1)} %bitcast.137, f32[8192,1024]{1,0:T(8,128)} %fusion.15, s32[]{:T(128)S(6)} %select_n.111), kind=kOutput, calls=%fused_computation.64 | convolution fusion | flops 2148532224 | bytes 10485764 | tf_op jit(solution)/shard_map/dot_general | solution.py:101
  1037.7 17.9 %fusion.36 = f32[1024,1024]{1,0:T(8,128)} fusion(f32[1024,1024]{1,0:T(8,128)S(1)} %fusion.34, bf16[1024,1024]{0,1:T(8,128)(2,1)S(1)} %bitcast.138, f32[8192,1024]{1,0:T(8,128)} %fusion.15, s32[]{:T(128)S(6)} %select_n.111), kind=kOutput, calls=%fused_computation.66 | convolution fusion | flops 2149580800 | bytes 14680068 | tf_op jit(solution)/shard_map/dot_general | solution.py:102
  1055.7 91.9 %reduce-scatter.3.cloned.1.call-done = f32[128,1024]{1,0:T(8,128)} async-done(((f32[1024,1024]{1,0:T(8,128)}), f32[128,1024]{1,0:T(8,128)}) %reduce-scatter.3.cloned.1.call-update) | async-done | bytes 524304 | tf_op jit(solution)/shard_map/reduce_scatter | solution.py:100
  1147.6 24.1 %reduce-scatter.5.cloned.1.call-done = f32[128,256]{1,0:T(8,128)} async-done(((f32[128,1024]{1,0:T(8,128)}), f32[128,256]{1,0:T(8,128)}) %reduce-scatter.5.cloned.1.call-update) | async-done | bytes 131088 | tf_op jit(solution)/shard_map/reduce_scatter | solution.py:107
  (67 shorter events, 19.4 us)
Async XLA Ops:
  49.4 35.8 %all-to-all-start = ((s32[8,1,96]{2,1,0:T(1,128)}), s32[8,1,96]{2,1,0:T(1,128)S(1)}, u32[]{:S(2)}, u32[]{:S(2)}) async-start(s32[8,1,96]{2,1,0:T(1,128)} %bitcast.27), calls=%async_computation | async-start | bytes 8192 | tf_op jit(solution)/shard_map/all_to_all | solution.py:65
  56.7 54.5 %copy-start.3 = (s32[1024]{0:T(1024)}, s32[1024]{0:T(1024)S(1)}, u32[]{:S(2)}) copy-start(s32[1024]{0:T(1024)S(1)} %add_multiply_fusion) | copy-start | bytes 12292
  85.2 27.8 %all-to-all-start.1 = ((f32[8,96,128]{2,1,0:T(8,128)}), f32[8,96,128]{2,1,0:T(8,128)S(1)}, u32[]{:S(2)}, u32[]{:S(2)}) async-start(f32[8,96,128]{2,1,0:T(8,128)} %scatter_fusion.2), calls=%async_computation.1 | async-start | bytes 786432 | tf_op jit(solution)/shard_map/all_to_all | solution.py:64
  91.3 1056.2 %reduce-scatter.3.cloned.1.call-start = ((), (), s32[]{:S(2)}) async-start(), calls=%async_computation.4 | async-start | bytes 4718592 | tf_op jit(solution)/shard_map/reduce_scatter | solution.py:100
  113.0 41.3 %copy-start = (bf16[1,32,2,64,128]{4,3,2,1,0:T(8,128)(2,1)S(1)}, bf16[1,32,2,64,128]{4,3,2,1,0:T(8,128)(2,1)}, u32[]{:S(2)}) copy-start(bf16[1,32,2,64,128]{4,3,2,1,0:T(8,128)(2,1)} %param.8) | copy-start | bytes 3145732
  162.9 9.0 slice-start
  163.0 8.9 slice-start.1
  262.5 9.0 slice-start
  262.6 8.9 slice-start.1
  362.4 9.0 slice-start
  362.5 8.9 slice-start.1
  518.2 105.0 %copy-start.2 = (s32[128,64]{0,1:T(8,128)S(1)}, s32[128,64]{0,1:T(8,128)}, u32[]{:S(2)}) copy-start(s32[128,64]{0,1:T(8,128)} %add_add_fusion) | copy-start | bytes 98308
  518.2 105.0 %copy-start.4 = (s32[1024]{0:T(1024)S(1)}, s32[1024]{0:T(1024)}, u32[]{:S(2)}) copy-start(s32[1024]{0:T(1024)} %copy-done.3) | copy-start | bytes 12292
  623.2 222.5 %copy-start.1 = (bf16[16,128,64,2,64]{1,2,4,3,0:T(8,128)(2,1)S(1)}, bf16[16,128,64,2,64]{1,2,4,3,0:T(8,128)(2,1)}, u32[]{:S(2)}) copy-start(bf16[16,128,64,2,64]{1,2,4,3,0:T(8,128)(2,1)} %copy.23) | copy-start | bytes 100663296
  1055.6 116.0 %reduce-scatter.5.cloned.1.call-start = ((), (), s32[]{:S(2)}) async-start(), calls=%async_computation.5 | async-start | bytes 655360 | tf_op jit(solution)/shard_map/reduce_scatter | solution.py:107
Sparse Core Ops, SparseCore 0:
  1055.7 91.7 reduce-scatter.2
  1150.2 21.4 reduce-scatter.4
where the time goes:
time: 1190 us; the launch traced here: 1180 us
  matrix products  472 us (40%)
  other arithmetic  323 us (27%)
  local copies, waits for them, and re-layouts  241 us (20%)
  waiting for transfers between devices  116 us (10%)
  between operations  13.9 us (1%)
  starting transfers between devices  13.5 us (1%)
    dot_general x1, matrix products, local(): jnp.einsum('acxpy,cym->pmax', grid_round, sine.reshape(cell_cols, S, P_SI...  223 us
    dot_general x1, matrix products, local(): jnp.einsum('acxpy,cym->pmax', grid_round, cosine.reshape(cell_cols, S, P_...  171 us
    scatter-add x3, other arithmetic, add_block(): return (grid_cells.at[meta_blk // NW].add(patches), None)  162 us
    reshape x1, local copies, waits for them, and re-layouts, local(): grid_cells.astype(jnp.bfloat16).reshape(slab_rows // S, cell_cols, S, 2, S)  105 us
    reduce_scatter x1, waiting for transfers between devices, local(): lax.psum_scatter(jnp.dot(transformed[0], own_cosine, preferred_element_ty...  91.9 us
    convert_element_type x1, other arithmetic, local(): grid_cells.astype(jnp.bfloat16).reshape(slab_rows // S, cell_cols, S, 2, S)  63.8 us
    dot_general x3, matrix products, block_patches(): jnp.einsum('bpkx,bpkqy->bxqy', u_kernel, v_weighted, preferred_element_ty...  44.3 us
    broadcast_in_dim x1, local copies, waits for them, and re-layouts, local(): grid_start = jnp.zeros((slab_rows // S * cell_cols, S, 2, S), jnp.float32)  41.3 us
  transfers between devices with their start and end apart: 4, of which 2 were waited for; matrix products, arithmetic and copies ran while one was open for 4% of the time, Pallas kernels for 0%

commit v1 on v0

v1 whole, which is shorter than its diff:
```python
import math

import jax
import jax.numpy as jnp
from jax import lax
from jax.sharding import PartitionSpec as P

G = 8192
S = 64
NW = 32
P_SIZE = 1024
NF = 8


def block_patches(samples, kernel_rows):
    sample_count = samples.shape[1] // 2
    support = kernel_rows.shape[3] // 2
    vis_real = samples[:, :sample_count, None]
    vis_imag = samples[:, sample_count:, None]
    kern_real = kernel_rows[:, 0, :, support:].astype(jnp.float32)
    kern_imag = kernel_rows[:, 1, :, support:].astype(jnp.float32)
    weighted_real = (vis_real * kern_real - vis_imag * kern_imag).astype(jnp.bfloat16)
    weighted_imag = (vis_real * kern_imag + vis_imag * kern_real).astype(jnp.bfloat16)
    u_kernel = kernel_rows[:, :, :, :support]
    v_weighted = jnp.stack(
        [
            jnp.stack([weighted_real, weighted_imag], 2),
            jnp.stack([-weighted_imag, weighted_real], 2),
        ],
        1,
    )
    return jnp.einsum("bpkx,bpkqy->bxqy", u_kernel, v_weighted, preferred_element_type=jnp.float32)


def phase_index(rows, cols):
    spacing = G // P_SIZE - 1
    return jnp.mod(rows[:, None] * (spacing * cols[None, :]), G)


def cos_sin(index):
    angle = index.astype(jnp.float32) * (2.0 * math.pi / G)
    return jnp.cos(angle).astype(jnp.bfloat16), jnp.sin(angle).astype(jnp.bfloat16)


def local(visibilities, kernels, destination, cell, plane):
    tile_count = lax.axis_size("tile")
    tile_index = lax.axis_index("tile")
    samples = visibilities[0]
    kernel_set = kernels[0]
    owners = destination[0, :, 0]
    blocks = samples.shape[0]
    capacity = 3 * blocks // tile_count
    spacing = G // P_SIZE - 1

    counts = jnp.sum(
        (owners[:, None] == jnp.arange(tile_count, dtype=jnp.int32)[None, :]).astype(jnp.int32), axis=0
    )
    first = jnp.cumsum(counts) - counts
    order = jnp.argsort(owners, stable=True).astype(jnp.int32)
    slot = jnp.arange(capacity, dtype=jnp.int32)
    valid = slot[None, :] < counts[:, None]
    src = order[jnp.clip(first[:, None] + slot[None, :], 0, blocks - 1)]
    packed_meta = cell[0] * NW + plane[0]
    send_samples = jnp.where(valid[:, :, None], samples[src], 0.0)
    send_meta = jnp.where(valid, packed_meta[src], 0)
    arrived = lax.all_to_all(send_samples, "tile", split_axis=0, concat_axis=0, tiled=True)
    arrived_meta = lax.all_to_all(send_meta, "tile", split_axis=0, concat_axis=0, tiled=True)
    slot_total = tile_count * capacity
    arrived = arrived.reshape(slot_total, samples.shape[1])
    arrived_meta = arrived_meta.reshape(slot_total)

    slab_rows = G // tile_count
    row_cells = slab_rows // S
    cell_cols = G // S
    q_len = G // NF
    q_cells = q_len // S
    j_len = P_SIZE // NF

    cell_r = arrived_meta // NW
    plane_r = arrived_meta % NW
    patches = block_patches(arrived, kernel_set[plane_r])
    rotated = jnp.stack([-patches[:, :, 1, :], patches[:, :, 0, :]], axis=2)
    p2 = jnp.stack([patches, rotated], axis=1).astype(jnp.bfloat16).reshape(slot_total, 2, S * 2 * S)

    a_s = cell_r // cell_cols
    cc_s = cell_r % cell_cols
    p_s = cc_s // q_cells
    qc_s = cc_s % q_cells
    resid = jnp.arange(NF, dtype=jnp.int32)
    ph_index = jnp.mod(spacing * (p_s[:, None] - NF // 2) * resid[None, :], NF)
    ph_angle = ph_index.astype(jnp.float32) * (2.0 * math.pi / NF)
    phase = jnp.stack([jnp.cos(ph_angle), jnp.sin(ph_angle)], axis=-1)
    place = (a_s[:, None] == jnp.arange(row_cells, dtype=jnp.int32)[None, :])[:, :, None] & (
        qc_s[:, None] == jnp.arange(q_cells, dtype=jnp.int32)[None, :]
    )[:, None, :]
    l2 = (place.astype(jnp.float32)[None, :, :, :, None] * jnp.transpose(phase, (1, 0, 2))[:, :, None, None, :])
    l2 = jnp.transpose(l2, (0, 2, 3, 1, 4)).astype(jnp.bfloat16)
    folded = jnp.einsum("raqsk,skn->raqn", l2, p2, preferred_element_type=jnp.float32).astype(jnp.bfloat16)
    folded = folded.reshape(NF, row_cells, q_cells, S, 2 * S)

    q_index = jnp.arange(q_len, dtype=jnp.int32)
    j_index = resid[:, None] + NF * (jnp.arange(j_len, dtype=jnp.int32)[None, :] - j_len // 2)
    idx1 = jnp.mod(q_index[None, :, None] * (spacing * j_index[:, None, :]), G)
    c1, s1 = cos_sin(idx1)
    w1 = jnp.stack([jnp.stack([c1, s1], axis=2), jnp.stack([-s1, c1], axis=2)], axis=2)
    w1 = w1.reshape(NF, q_cells, S, 2, 2, j_len)
    w1 = jnp.transpose(w1, (0, 1, 3, 2, 4, 5)).reshape(NF, q_cells, 2 * S, 2 * j_len)
    transformed = jnp.einsum("raqxk,rqkn->raxn", folded, w1, preferred_element_type=jnp.float32)
    transformed = transformed.astype(jnp.bfloat16).reshape(NF, slab_rows, 2, j_len)

    u_index = tile_index * slab_rows + jnp.arange(slab_rows, dtype=jnp.int32) - G // 2
    l_index = jnp.arange(P_SIZE, dtype=jnp.int32) - P_SIZE // 2
    c2, s2 = cos_sin(phase_index(u_index, l_index))
    e2 = jnp.stack([c2, -s2])
    partial = jnp.einsum("iul,ruij->lrj", e2, transformed, preferred_element_type=jnp.float32)
    partial = lax.psum_scatter(partial, "chan", scatter_dimension=0, tiled=True)
    partial = lax.psum_scatter(partial, "tile", scatter_dimension=2, tiled=True)
    out = jnp.transpose(partial, (0, 2, 1))
    return out.reshape(out.shape[0], -1) * (1.0 / G)


def solution(mesh):
    placed = (
        P("chan", "tile", None),
        P("chan", None, None, None, None),
        P("chan", "tile", None),
        P("chan", "tile"),
        P("chan", "tile"),
    )
    return jax.shard_map(
        local, mesh=mesh, in_specs=placed, out_specs=P("chan", "tile"), check_vma=False
    )
```

time: 1190 us -> 664 us (0.56)
  matrix products: 472 us -> 141 us
  other arithmetic: 323 us -> 193 us
  local copies, waits for them, and re-layouts: 241 us -> 190 us
    dot_general x4 -> x3, matrix products: 428 us -> 87.4 us  [the longest x1 59.5 us: local(): jnp.einsum('raqsk,skn->raqn', l2, p2, preferred_element_type=jnp.float32)]
    scatter-add x3 -> x0, other arithmetic: 162 us -> none  [add_block(): return (grid_cells.at[meta_blk // NW].add(patches), None)]
    another operation x1 -> x4, local copies, waits for them, and re-layouts: 0.01 us -> 90.3 us  [the longest x2 33 us: local(): jnp.stack([patches, rotated], axis=1).astype(jnp.bfloat16)]
    reshape x2 -> x4, local copies, waits for them, and re-layouts: 105 us -> 21.1 us  [the longest x1 14.1 us: local(): jnp.transpose(w1, (0, 1, 3, 2, 4, 5)).reshape(NF, q_cells, 2 * S, 2 * j_len)]
    scatter x2 -> x0, local copies, waits for them, and re-layouts: 66.3 us -> none  [the longest x1 38.6 us: local(): jnp.zeros((tile_count, capacity), jnp.int32).at[owners, slot_rank]]
    broadcast_in_dim x3 -> x0, local copies, waits for them, and re-layouts: 42.6 us -> none  [the longest x1 41.3 us: local(): grid_start = jnp.zeros((slab_rows // S * cell_cols, S, 2, S), jnp.float32)]
    neg x0 -> x2, other arithmetic: none -> 35.2 us  [the longest x1 17.6 us: local(): -s1]
    convert_element_type x2 -> x3, other arithmetic: 64.5 us -> 36.3 us  [the longest x1 18.8 us: cos_sin(): jnp.sin(angle).astype(jnp.bfloat16)]
  transfers between devices with their start and end apart: 4 -> 4, of which waited for: 2 -> 2; matrix products, arithmetic and copies ran while one was open for 4% -> 19% of each run, Pallas kernels for 0% -> 0%
where the time goes in v1:
time: 664 us; the launch traced here: 661 us
  other arithmetic  193 us (29%)
  local copies, waits for them, and re-layouts  190 us (29%)
  matrix products  141 us (21%)
  waiting for transfers between devices  111 us (17%)
  between operations  13.7 us (2%)
  starting transfers between devices  13.3 us (2%)
    reduce_scatter x1, waiting for transfers between devices, local(): partial = lax.psum_scatter(partial, 'tile', scatter_dimension=2, tiled=True)  64.6 us
    dot_general x1, matrix products, local(): jnp.einsum('raqsk,skn->raqn', l2, p2, preferred_element_type=jnp.float32)  59.5 us
    dot_general x1, matrix products, block_patches(): jnp.einsum('bpkx,bpkqy->bxqy', u_kernel, v_weighted, preferred_element_ty...  53.3 us
    reduce_scatter x1, waiting for transfers between devices, local(): partial = lax.psum_scatter(partial, 'chan', scatter_dimension=0, tiled=True)  46.5 us
    another operation x1, other arithmetic, block_patches(): jnp.stack([jnp.stack([weighted_real, weighted_imag], 2), jnp.stack([-weig...  33.2 us
    another operation x2, local copies, waits for them, and re-layouts, local(): jnp.stack([patches, rotated], axis=1).astype(jnp.bfloat16)  33 us
    another operation x1, local copies, waits for them, and re-layouts  28.6 us
    another operation x1, local copies, waits for them, and re-layouts, local(): rotated = jnp.stack([-patches[:, :, 1, :], patches[:, :, 0, :]], axis=2)  28.6 us
  transfers between devices with their start and end apart: 4, of which 2 were waited for; matrix products, arithmetic and copies ran while one was open for 19% of the time, Pallas kernels for 0%

profile of v1, /device:TPU:0, one launch (start us, length us, event | category | flops | bytes accessed | tf_op | source)
XLA Modules:
  0.0 661.5 jit_solution(15325599830670391448)
XLA Ops:
  7.8 3.8 sort.17
  11.6 5.0 gather_fusion
  17.5 5.0 gather_fusion.1
  23.2 7.3 %all-to-all-start = ((s32[8,1,96]{2,1,0:T(1,128)}), s32[8,1,96]{2,1,0:T(1,128)S(1)}, u32[]{:S(2)}, u32[]{:S(2)}) async-start(s32[8,1,96]{2,1,0:T(1,128)} %compare_select_fusion.1), calls=%async_computation | async-start | bytes 8192 | tf_op jit(solution)/shard_map/all_to_all | solution.py:67
  30.6 18.8 %sine_convert_fusion = (bf16[8,16,64,1,1,128]{5,2,4,3,1,0:T(8,128)(2,1)S(1)}, bf16[8,16,64,1,1,128]{5,2,4,3,1,0:T(8,128)(2,1)}) fusion(s32[8,128]{1,0:T(8,128)S(1)} %add_multiply_fusion, s32[16,64]{1,0:T(8,128)S(1)} %multiply_add_fusion), kind=kLoop, calls=%fused_computation.57 | loop fusion | flops 16777216 | bytes 4202496 | tf_op jit(solution)/shard_map/convert_element_type | solution.py:42
  49.4 17.6 %fusion.34 = bf16[8,16,64,1,1,128]{5,2,4,3,1,0:T(8,128)(2,1)} fusion(s32[8,128]{1,0:T(8,128)S(1)} %add_multiply_fusion, s32[16,64]{1,0:T(8,128)S(1)} %multiply_add_fusion), kind=kLoop, calls=%fused_computation.64 | loop fusion | flops 18874368 | bytes 2105344 | tf_op jit(solution)/shard_map/neg | solution.py:105
  67.0 17.4 %cosine_convert_fusion.1 = bf16[1,1024,1024]{1,2,0:T(8,128)(2,1)} fusion(s32[1024]{0:T(1024)S(1)} %get-tuple-element.24, s32[1024]{0:T(1024)S(1)} %get-tuple-element.25), kind=kLoop, calls=%fused_computation.60 | loop fusion | flops 15728640 | bytes 2105344 | tf_op jit(solution)/shard_map/convert_element_type | solution.py:42
  84.5 17.6 %fusion.33 = bf16[1,1024,1024]{1,2,0:T(8,128)(2,1)} fusion(s32[1024]{0:T(1024)S(1)} %get-tuple-element.24, s32[1024]{0:T(1024)S(1)} %get-tuple-element.25), kind=kLoop, calls=%fused_computation.62 | loop fusion | flops 18874368 | bytes 2105344 | tf_op jit(solution)/shard_map/neg | solution.py:114
  104.3 4.1 maximum_bitcast_fusion.4
  109.4 7.8 %copy.63 = bf16[8,16,2,64,2,128]{5,4,3,2,1,0:T(2,128)(2,1)} copy(bf16[8,16,2,64,2,128]{5,3,4,2,1,0:T(8,128)(2,1)S(1)} %maximum_bitcast_fusion.4) | data formatting | bytes 16777216 | tf_op jit(solution)/shard_map/transpose | solution.py:107
  117.2 14.1 %reshape.838 = bf16[8,16,128,256,1]{3,2,1,0,4:T(8,128)(2,1)} reshape(bf16[8,16,2,64,2,128]{5,4,3,2,1,0:T(2,128)(2,1)} %copy.63) | data formatting | bytes 16777216 | tf_op jit(solution)/shard_map/reshape | solution.py:107
  131.3 6.0 all-to-all-start.1
  138.9 18.9 %gather_fusion.2 = bf16[768,2,64,128]{3,2,1,0:T(8,128)(2,1)} fusion(bf16[32,2,64,128]{3,2,1,0:T(8,128)(2,1)S(1)} %bitcast.104, s32[1024]{0:T(1024)S(1)} %pad_clamp_fusion), kind=kCustom, calls=%fused_computation.2 | custom fusion | bytes 50334720 | tf_op jit(solution)/shard_map/gather | solution.py:81
  157.9 4.6 multiply_convert_fusion.5
  162.7 25.6 %fusion.56 = (bf16[768,64,1,64]{3,1,2,0:T(8,128)(2,1)}, bf16[768,64,1,64]{3,1,2,0:T(8,128)(2,1)}) fusion(bf16[768,2,64,128]{3,2,1,0:T(8,128)(2,1)} %gather_fusion.2, f32[768,64]{1,0:T(8,128)S(1)} %get-tuple-element.12, f32[768,64]{1,0:T(8,128)S(1)} %get-tuple-element.11), kind=kLoop, calls=%fused_computation.131 | loop fusion | flops 22020096 | bytes 25559040 | tf_op jit(solution)/shard_map/neg | solution.py:28
  188.4 23.0 %fusion.5 = bf16[768,64,1,64]{3,1,2,0:T(8,128)(2,1)} fusion(f32[768,64]{1,0:T(8,128)S(1)} %get-tuple-element.12, f32[768,64]{1,0:T(8,128)S(1)} %get-tuple-element.11, bf16[768,2,64,128]{3,2,1,0:T(8,128)(2,1)S(1)} %bitcast.107), kind=kLoop, calls=%fused_computation.14 | loop fusion | flops 18874368 | bytes 19267584 | tf_op jit(solution)/shard_map/convert_element_type | solution.py:22
  211.4 33.2 %maximum_bitcast_fusion = (bf16[768,1,64,2,64]{4,2,1,3,0:T(8,128)(2,1)}, bf16[768,1,64,2,64]{4,2,1,3,0:T(8,128)(2,1)}) fusion(bf16[768,64,1,64]{3,1,2,0:T(8,128)(2,1)} %get-tuple-element.8, bf16[768,64,1,64]{3,1,2,0:T(8,128)(2,1)} %fusion.5, bf16[768,64,1,64]{3,1,2,0:T(8,128)(2,1)} %get-tuple-element.7), kind=kLoop, calls=%fused_computation.20 | loop fusion | flops 12582912 | bytes 44040192 | tf_op jit(solution)/shard_map/stack | solution.py:25
  244.6 53.3 %fusion.59 = (bf16[768,64,2,64]{3,1,2,0:T(8,128)(2,1)}, f32[768,64,2,64]{3,1,2,0:T(8,128)}) fusion(bf16[768,1,64,2,64]{4,2,1,3,0:T(8,128)(2,1)} %get-tuple-element.10, bf16[768,1,64,2,64]{4,2,1,3,0:T(8,128)(2,1)} %get-tuple-element.9, bf16[768,2,64,128]{3,2,1,0:T(8,128)(2,1)} %gather_fusion.2), kind=kOutput, calls=%fused_computation.133 | convolution fusion | flops 1667235840 | bytes 88080384 | tf_op jit(solution)/shard_map/bpkx,bpkqy->bxqy/dot_general | solution.py:32
  298.0 10.5 %slice.43 = bf16[768,64,1,64]{3,1,2,0:T(8,128)(2,1)} slice(bf16[768,64,2,64]{3,1,2,0:T(8,128)(2,1)} %get-tuple-element.20), slice={[0:768], [0:64], [0:1], [0:64]} | slice | bytes 12582912 | tf_op jit(solution)/shard_map/slice | solution.py:82
  308.5 28.6 %copy.59 = bf16[768,64,2,64]{0,3,2,1:T(8,128)(2,1)} copy(bf16[768,64,2,64]{3,1,2,0:T(8,128)(2,1)} %get-tuple-element.20) | data formatting | bytes 25165824 | tf_op jit(solution)/shard_map/convert.8
  337.1 10.4 %fusion.8 = bf16[768,64,1,64]{3,1,2,0:T(8,128)(2,1)S(1)} fusion(f32[768,64,2,64]{3,1,2,0:T(8,128)} %get-tuple-element.21), kind=kLoop, calls=%fused_computation.18 | loop fusion | flops 6291456 | bytes 18874368 | tf_op jit(solution)/shard_map/convert.5
  349.0 11.1 %pad_maximum_fusion = bf16[768,64,2,64]{3,1,2,0:T(8,128)(2,1)} fusion(bf16[768,64,1,64]{3,1,2,0:T(8,128)(2,1)S(1)} %copy-done.3, bf16[768,64,1,64]{3,1,2,0:T(8,128)(2,1)S(1)} %fusion.8), kind=kLoop, calls=%fused_computation.22 | loop fusion | flops 6291456 | bytes 25165824 | tf_op jit(solution)/shard_map/stack | solution.py:82
  360.1 28.6 %copy.60 = bf16[768,64,2,64]{0,3,2,1:T(8,128)(2,1)} copy(bf16[768,64,2,64]{3,1,2,0:T(8,128)(2,1)} %pad_maximum_fusion) | data formatting | bytes 25165824 | tf_op jit(solution)/shard_map/stack | solution.py:82
  388.7 16.7 %copy.62 = bf16[768,1,8192]{2,0,1:T(8,128)(2,1)} copy(bf16[768,1,8192]{0,2,1:T(8,128)(2,1)} %bitcast.110) | data formatting | bytes 25165824 | tf_op jit(solution)/shard_map/stack | solution.py:83
  405.4 16.3 %copy.61 = bf16[768,1,8192]{2,0,1:T(8,128)(2,1)} copy(bf16[768,1,8192]{0,2,1:T(8,128)(2,1)} %bitcast.109) | data formatting | bytes 25165824 | tf_op jit(solution)/shard_map/stack | solution.py:83
  421.7 59.5 %bitcast_convert_fusion = bf16[8,16,16,8192]{3,2,1,0:T(8,128)(2,1)} fusion(bf16[768,1,8192]{2,0,1:T(8,128)(2,1)} %copy.62, bf16[768,1,8192]{2,0,1:T(8,128)(2,1)} %copy.61, bf16[8,16,16,768,2]{3,2,4,1,0:T(8,128)(2,1)} %multiply_convert_fusion.5), kind=kOutput, calls=%fused_computation.4 | convolution fusion | flops 51568967680 | bytes 65011712 | tf_op jit(solution)/shard_map/raqsk,skn->raqn/dot_general | solution.py:98
  481.3 23.1 %copy.77 = bf16[256,8,64,128]{3,2,1,0:T(8,128)(2,1)} copy(bf16[256,8,64,128]{3,1,2,0:T(8,128)(2,1)} %bitcast.111) | data formatting | bytes 67108864
  504.3 18.5 %bitcast_convert_fusion.1 = bf16[8,16,64,256]{3,2,1,0:T(8,128)(2,1)} fusion(bf16[8,16,16,64,128]{4,3,2,1,0:T(8,128)(2,1)} %bitcast.112, bf16[8,16,128,256,1]{3,2,1,0,4:T(8,128)(2,1)} %reshape.838), kind=kOutput, calls=%fused_computation.31 | convolution fusion | flops 8592031744 | bytes 46137344 | tf_op jit(solution)/shard_map/raqxk,rqkn->raxn/dot_general | solution.py:108
  522.8 6.9 %reshape.794 = bf16[8,1024,2,128]{3,2,1,0:T(2,128)(2,1)} reshape(bf16[8,16,64,256]{3,2,1,0:T(8,128)(2,1)} %bitcast_convert_fusion.1) | data formatting | bytes 8388608 | tf_op jit(solution)/shard_map/reshape | solution.py:109
  529.7 9.4 %fusion.30 = f32[1024,8,128]{2,0,1:T(8,128)} fusion(bf16[8,1024,2,128]{3,2,1,0:T(2,128)(2,1)} %reshape.794, bf16[1,1024,1024]{1,2,0:T(8,128)(2,1)} %fusion.33, bf16[1,1024,1024]{1,2,0:T(8,128)(2,1)S(1)} %copy-done.4), kind=kOutput, calls=%fused_computation.61 | convolution fusion | flops 4303355904 | bytes 12582912 | tf_op jit(solution)/shard_map/iul,ruij->lrj/dot_general | solution.py:115
  539.2 46.5 %reduce-scatter.3.cloned.1.call-done = f32[256,8,128]{2,0,1:T(8,128)} async-done(((f32[1024,8,128]{2,0,1:T(8,128)}), f32[256,8,128]{2,0,1:T(8,128)}) %reduce-scatter.3.cloned.1.call-update) | async-done | bytes 1048592 | tf_op jit(solution)/shard_map/reduce_scatter | solution.py:116
  588.3 64.6 %reduce-scatter.5.cloned.1.call-done = f32[256,8,16]{0,1,2:T(8,128)} async-done(((f32[256,8,128]{0,1,2:T(8,128)}), f32[256,8,16]{0,1,2:T(8,128)}) %reduce-scatter.5.cloned.1.call-update) | async-done | bytes 131088 | tf_op jit(solution)/shard_map/reduce_scatter | solution.py:117
  (68 shorter events, 13.9 us)
Async XLA Ops:
  6.5 132.4 %copy-start = (bf16[1,32,2,64,128]{4,3,2,1,0:T(8,128)(2,1)S(1)}, bf16[1,32,2,64,128]{4,3,2,1,0:T(8,128)(2,1)}, u32[]{:S(2)}) copy-start(bf16[1,32,2,64,128]{4,3,2,1,0:T(8,128)(2,1)} %param.6) | copy-start | bytes 3145732
  16.6 85.5 %copy-start.2 = (f32[1,256,128]{2,1,0:T(8,128)S(1)}, f32[1,256,128]{2,1,0:T(8,128)}, u32[]{:S(2)}) copy-start(f32[1,256,128]{2,1,0:T(8,128)} %param.5) | copy-start | bytes 393220
  23.2 108.1 %all-to-all-start = ((s32[8,1,96]{2,1,0:T(1,128)}), s32[8,1,96]{2,1,0:T(1,128)S(1)}, u32[]{:S(2)}, u32[]{:S(2)}) async-start(s32[8,1,96]{2,1,0:T(1,128)} %compare_select_fusion.1), calls=%async_computation | async-start | bytes 8192 | tf_op jit(solution)/shard_map/all_to_all | solution.py:67
  104.3 4.1 copy-start.5
  131.3 31.2 %all-to-all-start.1 = ((f32[8,96,128]{2,1,0:T(8,128)}), f32[8,96,128]{2,1,0:T(8,128)S(1)}, u32[]{:S(2)}, u32[]{:S(2)}) async-start(f32[8,96,128]{2,1,0:T(8,128)} %broadcast_select_fusion), calls=%async_computation.1 | async-start | bytes 786432 | tf_op jit(solution)/shard_map/all_to_all | solution.py:66
  137.3 448.4 %reduce-scatter.3.cloned.1.call-start = ((), (), s32[]{:S(2)}) async-start(), calls=%async_computation.4 | async-start | bytes 5242880 | tf_op jit(solution)/shard_map/reduce_scatter | solution.py:116
  162.5 25.9 %slice-start = ((s8[25165824]{0:T(1024)(128)(4,1)}), s8[4194304]{0:T(1024)(128)(4,1)S(1)}, s32[]{:S(2)}) async-start(s8[25165824]{0:T(1024)(128)(4,1)} %bitcast.106), calls=%async_computation.6 | async-start | bytes 8388608
  162.7 25.7 %slice-start.1 = ((s8[25165824]{0:T(1024)(128)(4,1)}), s8[4194304]{0:T(1024)(128)(4,1)S(1)}, s32[]{:S(2)}) async-start(s8[25165824]{0:T(1024)(128)(4,1)} %bitcast.106), calls=%async_computation.7 | async-start | bytes 8388608
  162.7 25.7 %slice-start.2 = ((s8[25165824]{0:T(1024)(128)(4,1)}), s8[4194304]{0:T(1024)(128)(4,1)S(1)}, s32[]{:S(2)}) async-start(s8[25165824]{0:T(1024)(128)(4,1)} %bitcast.106), calls=%async_computation.8 | async-start | bytes 8388608
  162.7 25.7 %slice-start.3 = ((s8[25165824]{0:T(1024)(128)(4,1)}), s8[4194304]{0:T(1024)(128)(4,1)S(1)}, s32[]{:S(2)}) async-start(s8[25165824]{0:T(1024)(128)(4,1)} %bitcast.106), calls=%async_computation.9 | async-start | bytes 8388608
  162.7 25.7 %slice-start.4 = ((s8[25165824]{0:T(1024)(128)(4,1)}), s8[4194304]{0:T(1024)(128)(4,1)S(1)}, s32[]{:S(2)}) async-start(s8[25165824]{0:T(1024)(128)(4,1)} %bitcast.106), calls=%async_computation.10 | async-start | bytes 8388608
  162.7 25.7 %slice-start.5 = ((s8[25165824]{0:T(1024)(128)(4,1)}), s8[4194304]{0:T(1024)(128)(4,1)S(1)}, s32[]{:S(2)}) async-start(s8[25165824]{0:T(1024)(128)(4,1)} %bitcast.106), calls=%async_computation.11 | async-start | bytes 8388608
  337.1 11.9 %copy-start.3 = (bf16[768,64,1,64]{3,1,2,0:T(8,128)(2,1)S(1)}, bf16[768,64,1,64]{3,1,2,0:T(8,128)(2,1)}, u32[]{:S(2)}) copy-start(bf16[768,64,1,64]{3,1,2,0:T(8,128)(2,1)} %slice.43) | copy-start | bytes 18874372
  504.3 25.4 %copy-start.4 = (bf16[1,1024,1024]{1,2,0:T(8,128)(2,1)S(1)}, bf16[1,1024,1024]{1,2,0:T(8,128)(2,1)}, u32[]{:S(2)}) copy-start(bf16[1,1024,1024]{1,2,0:T(8,128)(2,1)} %cosine_convert_fusion.1) | copy-start | bytes 6291460
  529.7 124.9 %copy-start.1 = (bf16[1,32,2,64,128]{4,3,2,1,0:T(8,128)(2,1)S(1)}, bf16[1,32,2,64,128]{4,3,2,1,0:T(8,128)(2,1)}, u32[]{:S(2)}) copy-start(bf16[1,32,2,64,128]{4,3,2,1,0:T(8,128)(2,1)} %param.6) | copy-start | bytes 3145732
  539.1 113.8 %reduce-scatter.5.cloned.1.call-start = ((), (), s32[]{:S(2)}) async-start(), calls=%async_computation.5 | async-start | bytes 1179648 | tf_op jit(solution)/shard_map/reduce_scatter | solution.py:117
Sparse Core Ops, SparseCore 0:
  539.2 46.3 reduce-scatter.2
  589.5 63.4 reduce-scatter.4
